TPU v7x, 32 devices: a whole 2x2x4 slice. The times are simulated.
32 devices in a mesh: ctx: 16 (over z, y, core), head: 2 (over x).
Axes of the slice: x: 2, y: 2, z: 4, core: 2. Of those that a mesh axis runs over, the one named last changes fastest.
Arguments:
- queries: bfloat16 [2048, 1536], P('ctx', 'head'), may hold values from -45 to 45
- key_rows: bfloat16 [2048, 256], P('ctx', 'head'), may hold values from -5 to 5
- value_rows: bfloat16 [2048, 256], P('ctx', 'head'), may hold values from -18 to 18
- cotangent: bfloat16 [2048, 1536], P('ctx', 'head'), may hold values from -6 to 6
- trace_ids: int32 [2048], P('ctx'), may hold values from 0 to 15, never falling along the last dimension, each value on 1 to 512 neighbouring positions
- correct: int32 [16], replicated, may hold values from 0 to 16, as said below
- group_size: int32 [16], replicated, may hold values from 4 to 16
Outputs:
- log_totals: float32 [2048, 12], P('ctx', 'head')
- grad_queries: float32 [2048, 1536], P('ctx', 'head')
- grad_keys: bfloat16 [2048, 256], P('ctx', 'head')
- grad_values: bfloat16 [2048, 256], P('ctx', 'head')
Inputs may be any that keep to these rules, and one draw needn't show every extreme that they name: correct[g] is at most group_size[g].
All inputs are finite; a program needn't handle non-finite values.
Results may differ from a plain program's by a relative error of at most 0.0054.
Values may be sent and summed in bfloat16 or wider, within the bound.
No kernel may reach another device: no remote copies, remote signals or barrier semaphores. Data moves between devices by JAX's collectives and lax.ppermute only.
A program may use at most 64 MiB of HBM per device.

v0:
```python
import math
import jax
import jax.numpy as jnp
from jax import lax
from jax.sharding import PartitionSpec as P

PASSK = 4


def pass_rate(correct, group_size):
    counts = group_size.astype(jnp.float32)
    hit_counts = correct.astype(jnp.float32)
    product = jnp.ones_like(counts)
    for offset in range(PASSK):
        product = product * (counts - hit_counts - offset) / (counts - offset)
    return 1.0 - product


def body(queries, key_rows, value_rows, cotangent, trace_ids, correct, group_size):
    tok_rows = queries.shape[0]
    half_rows = tok_rows // 2
    row_width = queries.shape[1]
    head_dim = key_rows.shape[1]
    head_count = row_width // head_dim
    ctx_count = lax.axis_size("ctx")
    my_index = lax.axis_index("ctx")
    length = tok_rows * ctx_count
    score_scale = 1.0 / math.sqrt(head_dim)
    pass_rates = pass_rate(correct, group_size)
    traces = jnp.arange(pass_rates.shape[0], dtype=jnp.int32)
    weights = jnp.sum(
        jnp.where(trace_ids[:, None] == traces[None, :], pass_rates[None, :], 0.0), axis=1
    )
    out_grads = (weights[:, None] * cotangent.astype(jnp.float32)).astype(jnp.bfloat16)
    first_base = my_index * tok_rows
    second_base = first_base + half_rows
    local_pos = jnp.arange(half_rows, dtype=jnp.int32)
    positions = jnp.concatenate([first_base + local_pos, second_base + local_pos], 0)
    last_first = first_base + half_rows - 1
    last_second = second_base + half_rows - 1
    query_all = queries.reshape(tok_rows, head_count, head_dim)
    grad_all = out_grads.reshape(tok_rows, head_count, head_dim)

    def run_block(running, key_block, value_block, key_start, block_fn):
        need_first = (key_start <= last_first).astype(jnp.int32)
        need_second = (key_start <= last_second).astype(jnp.int32)
        branch_index = need_first + 2 * need_second

        def skip_block(values_in):
            return values_in

        def first_only(values_in):
            return block_fn((0, half_rows), values_in, key_block, value_block, key_start)

        def second_only(values_in):
            return block_fn((half_rows, tok_rows), values_in, key_block, value_block, key_start)

        def both_halves(values_in):
            return block_fn((0, tok_rows), values_in, key_block, value_block, key_start)

        return lax.switch(branch_index, [skip_block, first_only, second_only, both_halves], running)

    def forward_block(row_span, running, key_block, value_block, key_start):
        row_begin, row_end = row_span
        row_peak, row_total, weighted = running
        query_part = query_all[row_begin:row_end]
        grad_part = grad_all[row_begin:row_end]
        query_pos = positions[row_begin:row_end]
        scores = (
            jnp.einsum("tqd,kd->tqk", query_part, key_block, preferred_element_type=jnp.float32)
            * score_scale
        )
        key_pos = key_start + jnp.arange(key_block.shape[0], dtype=jnp.int32)
        visible = key_pos[None, None, :] <= query_pos[:, None, None]
        block_peak = jnp.max(jnp.where(visible, scores, -1e30), axis=2)
        old_peak = row_peak[row_begin:row_end]
        new_peak = jnp.maximum(old_peak, block_peak)
        exp_terms = jnp.where(visible, jnp.exp(scores - new_peak[:, :, None]), 0.0)
        grad_probs = jnp.einsum(
            "tqd,kd->tqk", grad_part, value_block, preferred_element_type=jnp.float32
        )
        shrink = jnp.exp(old_peak - new_peak)
        new_total = row_total[row_begin:row_end] * shrink + jnp.sum(exp_terms, axis=2)
        new_weighted = weighted[row_begin:row_end] * shrink + jnp.sum(
            exp_terms * grad_probs, axis=2
        )
        return (
            row_peak.at[row_begin:row_end].set(new_peak),
            row_total.at[row_begin:row_end].set(new_total),
            weighted.at[row_begin:row_end].set(new_weighted),
        )

    row_peak = jnp.full((tok_rows, head_count), -1e30, jnp.float32)
    row_total = jnp.zeros((tok_rows, head_count), jnp.float32)
    weighted = jnp.zeros((tok_rows, head_count), jnp.float32)
    key_piece = lax.all_gather(key_rows, "ctx", axis=0, tiled=True)
    value_piece = lax.all_gather(value_rows, "ctx", axis=0, tiled=True)
    piece_rows = key_piece.shape[0]
    block_rows = math.gcd(piece_rows, 512)

    def forward_step(step_index, statistics):
        offset = step_index * block_rows
        key_block = lax.dynamic_slice_in_dim(key_piece, offset, block_rows, 0)
        value_block = lax.dynamic_slice_in_dim(value_piece, offset, block_rows, 0)
        return run_block(statistics, key_block, value_block, offset, forward_block)

    statistics = lax.fori_loop(
        0, piece_rows // block_rows, forward_step, (row_peak, row_total, weighted)
    )
    folded = statistics + (key_piece, value_piece)
    row_peak, row_total, weighted, key_store, value_store = folded
    log_totals = row_peak + jnp.log(row_total)
    delta_rows = weighted / row_total

    def backward_block(row_span, running, key_block, value_block, key_start):
        row_begin, row_end = row_span
        grad_query, zero_block = running
        query_part = query_all[row_begin:row_end]
        grad_part = grad_all[row_begin:row_end]
        query_pos = positions[row_begin:row_end]
        scores = (
            jnp.einsum("tqd,kd->tqk", query_part, key_block, preferred_element_type=jnp.float32)
            * score_scale
        )
        key_pos = key_start + jnp.arange(key_block.shape[0], dtype=jnp.int32)
        visible = key_pos[None, None, :] <= query_pos[:, None, None]
        probabilities = jnp.where(
            visible, jnp.exp(scores - log_totals[row_begin:row_end][:, :, None]), 0.0
        )
        prob_bf16 = probabilities.astype(jnp.bfloat16)
        grad_probs = jnp.einsum(
            "tqd,kd->tqk", grad_part, value_block, preferred_element_type=jnp.float32
        )
        grad_scores = (
            probabilities * (grad_probs - delta_rows[row_begin:row_end][:, :, None])
        ).astype(jnp.bfloat16)
        query_add = (
            jnp.einsum("tqk,kd->tqd", grad_scores, key_block, preferred_element_type=jnp.float32)
            * score_scale
        )
        key_add = (
            jnp.einsum("tqk,tqd->kd", grad_scores, query_part, preferred_element_type=jnp.float32)
            * score_scale
        )
        value_add = jnp.einsum(
            "tqk,tqd->kd", prob_bf16, grad_part, preferred_element_type=jnp.float32
        )
        return (
            grad_query.at[row_begin:row_end].add(query_add),
            jnp.concatenate([key_add, value_add], 1),
        )

    query_zero = jnp.zeros((tok_rows, head_count, head_dim), jnp.float32)
    key_block_rows = math.gcd(length, 512)

    def backward_step(step_index, running):
        grad_query, partial_sums = running
        key_start = step_index * key_block_rows
        key_block = lax.dynamic_slice_in_dim(key_store, key_start, key_block_rows, 0)
        value_block = lax.dynamic_slice_in_dim(value_store, key_start, key_block_rows, 0)
        zero_block = jnp.zeros((key_block_rows, 2 * head_dim), jnp.float32)
        grad_query, block_sums = run_block(
            (grad_query, zero_block), key_block, value_block, key_start, backward_block
        )
        partial_sums = lax.dynamic_update_slice_in_dim(partial_sums, block_sums, key_start, 0)
        return (grad_query, partial_sums)

    grad_query, partial_sums = lax.fori_loop(
        0,
        length // key_block_rows,
        backward_step,
        (query_zero, jnp.zeros((length, 2 * head_dim), jnp.float32)),
    )
    reduced = jnp.sum(
        lax.all_to_all(
            partial_sums.reshape(ctx_count, tok_rows, 2 * head_dim),
            "ctx",
            split_axis=0,
            concat_axis=0,
            tiled=True,
        ),
        axis=0,
    )
    grad_keys = reduced[:, :head_dim].astype(jnp.bfloat16)
    grad_values = reduced[:, head_dim:].astype(jnp.bfloat16)
    query_grads = grad_query.reshape(tok_rows, row_width)
    return (log_totals, query_grads, grad_keys, grad_values)


def solution(mesh):
    return jax.shard_map(
        body,
        mesh=mesh,
        in_specs=(
            P("ctx", "head"),
            P("ctx", "head"),
            P("ctx", "head"),
            P("ctx", "head"),
            P("ctx"),
            P(),
            P(),
        ),
        out_specs=(P("ctx", "head"), P("ctx", "head"), P("ctx", "head"), P("ctx", "head")),
        check_vma=False,
    )
```

profile of v0, /device:TPU:13, one launch (start us, length us, event | category | flops | bytes accessed | tf_op | source)
XLA Modules:
  0.0 124.0 jit_solution(4631487437105801853)
XLA Ops:
  0.7 0.7 fusion.61
  1.4 0.7 select_reduce_fusion.3
  2.1 1.0 multiply_convert_fusion.1
  3.1 0.2 copy.73
  3.3 0.2 copy.75
  3.5 1.1 copy.72
  4.6 0.2 copy.74
  4.8 17.1 %all_gather.6 = bf16[2048,128]{1,0:T(8,128)(2,1)S(1)} all-gather(bf16[128,128]{1,0:T(8,128)(2,1)S(1)} %copy-done.1), channel_id=1, replica_groups=mesh['ctx'=16,'head'=2] {'ctx'}, dimensions={0}, use_global_device_ids=true | all-gather | bytes 557056 | tf_op jit(solution)/shard_map/all_gather | solution.py:96
  21.9 22.8 %all_gather.7 = bf16[2048,128]{1,0:T(8,128)(2,1)S(1)} all-gather(bf16[128,128]{1,0:T(8,128)(2,1)S(1)} %copy-done.2), channel_id=1, replica_groups=mesh['ctx'=16,'head'=2] {'ctx'}, dimensions={0}, use_global_device_ids=true | all-gather | bytes 557056 | tf_op jit(solution)/shard_map/all_gather | solution.py:97
  44.8 3.9 %while.53 = (s32[]{:T(128)}, f32[128,6]{0,1:T(8,128)S(1)}, f32[128,6]{0,1:T(8,128)S(1)}, f32[128,6]{0,1:T(8,128)S(1)}, s32[]{:T(128)}, /*index=5*/s32[]{:T(128)}...) while((s32[]{:T(128)}, f32[128,6]{0,1:T(8,128)S(1)}, ...), condition=%wide.region_15.0_spmd.clone, body=%wide.region_1.15_spmd.clone.sunk | while | flops 205327120 | bytes 6221379 | solution.py:107
  44.8 1.7 %conditional.6 = ((f32[128,6]{0,1:T(8,128)S(1)}, f32[128,6]{0,1:T(8,128)S(1)}, f32[128,6]{0,1:T(8,128)S(1)})) conditional(s32[]{:T(128)} %clamp.18, (f32[128,6]{0,1:T(8,128)S(1)}, f32[128,6]{0,1:T(8,128)S(1)}, f32[128,6]{0,1:T(8,128)S(1)}) %tuple.202, (f32[128,6]{0,1:T(8,128)S(1)}, s32[]{:T(128)}, s32[]{:T(128)}, ...), branch_computations={%region_2.2_spmd, %region_3.6_spmd, %region_7.10_spmd, %region_11.... | conditional | flops 205327104 | bytes 5696036 | solution.py:61
  44.9 0.1 broadcast_compare_fusion.2
  45.0 0.5 select_reduce_fusion.2
  45.4 0.6 multiply_reduce_fusion
  46.0 0.5 fusion.20
  46.6 1.7 %conditional.6 = ((f32[128,6]{0,1:T(8,128)S(1)}, f32[128,6]{0,1:T(8,128)S(1)}, f32[128,6]{0,1:T(8,128)S(1)})) conditional(s32[]{:T(128)} %clamp.18, (f32[128,6]{0,1:T(8,128)S(1)}, f32[128,6]{0,1:T(8,128)S(1)}, f32[128,6]{0,1:T(8,128)S(1)}) %tuple.202, (f32[128,6]{0,1:T(8,128)S(1)}, s32[]{:T(128)}, s32[]{:T(128)}, ...), branch_computations={%region_2.2_spmd, %region_3.6_spmd, %region_7.10_spmd, %region_11.... | conditional | flops 205327104 | bytes 5696036 | solution.py:61
  46.8 0.5 select_reduce_fusion.2
  47.3 0.6 multiply_reduce_fusion
  47.8 0.5 fusion.20
  48.7 1.5 %broadcast_in_dim.124.clone = f32[2048,256]{1,0:T(8,128)} broadcast(f32[]{:T(128)} %constant.488.clone.1), dimensions={} | broadcast | bytes 2097156 | tf_op jit(solution)/shard_map/broadcast_in_dim | solution.py:172
  50.2 8.7 %while.54 = (s32[]{:T(128)}, f32[128,6,128]{2,0,1:T(8,128)S(1)}, f32[2048,256]{1,0:T(8,128)}, s32[]{:T(128)}, s32[]{:T(128)}, /*index=5*/bf16[2048,128]{1,0:T(8,...) while((s32[]{:T(128)}, f32[128,6,128]{2,0,1:T(8,128)S(1)}, ...), condition=%wide.region_21.22_spmd.clone, body=%wide.region_16.21_spmd.clone.sunk | while | flops 506528256 | bytes 13381159 | solution.py:168
  50.2 2.1 %conditional.7 = (f32[128,6,128]{2,0,1:T(8,128)S(1)}, f32[512,256]{0,1:T(8,128)S(1)}) conditional(s32[]{:T(128)} %clamp.19, f32[128,6,128]{2,0,1:T(8,128)S(1)} %get-tuple-element.1421, (f32[128,6,128]{2,0,1:T(8,128)S(1)}, s32[]{:T(128)}, s32[]{:T(128)}, bf16[128,6,128]{0,2,1:T(8,128)(2,1)S(1)}, ...), branch_computations={%region_17.17_spmd, %region_18.18_spmd, %region_19.19_spmd, %regio... | conditional | flops 506528256 | bytes 10758676 | solution.py:61
  50.4 0.5 exponential_select_fusion.3
  50.9 0.3 convolution_bitcast_fusion.4
  51.2 0.4 multiply_convert_fusion
  51.6 0.3 fusion.56
  51.9 0.4 fusion.55
  52.3 0.2 copy.91
  52.5 0.8 constant_dynamic-update-slice_fusion.2
  53.4 2.1 %conditional.7 = (f32[128,6,128]{2,0,1:T(8,128)S(1)}, f32[512,256]{0,1:T(8,128)S(1)}) conditional(s32[]{:T(128)} %clamp.19, f32[128,6,128]{2,0,1:T(8,128)S(1)} %get-tuple-element.1421, (f32[128,6,128]{2,0,1:T(8,128)S(1)}, s32[]{:T(128)}, s32[]{:T(128)}, bf16[128,6,128]{0,2,1:T(8,128)(2,1)S(1)}, ...), branch_computations={%region_17.17_spmd, %region_18.18_spmd, %region_19.19_spmd, %regio... | conditional | flops 506528256 | bytes 10758676 | solution.py:61
  53.5 0.5 exponential_select_fusion.3
  54.1 0.3 convolution_bitcast_fusion.4
  54.3 0.4 multiply_convert_fusion
  54.8 0.3 fusion.56
  55.0 0.4 fusion.55
  55.5 0.2 copy.91
  55.7 0.9 constant_dynamic-update-slice_fusion.2
  56.7 0.2 copy.91
  56.9 0.9 constant_dynamic-update-slice_fusion.2
  57.8 0.2 copy.91
  58.1 0.9 constant_dynamic-update-slice_fusion.2
  58.9 2.9 %copy.78 = f32[16,128,256]{1,2,0:T(8,128)} copy(f32[16,128,256]{2,1,0:T(8,128)} %bitcast.88) | data formatting | bytes 4194304 | tf_op jit(solution)/shard_map/reshape | solution.py:176
  61.8 13.2 %all-to-all-start = ((f32[16,128,256]{1,2,0:T(8,128)}), f32[16,128,256]{1,2,0:T(8,128)S(1)}, u32[]{:S(2)}, u32[]{:S(2)}) async-start(f32[16,128,256]{1,2,0:T(8,128)} %copy.78), calls=%async_computation | async-start | bytes 4194304 | tf_op jit(solution)/shard_map/all_to_all | solution.py:175
  75.0 0.2 copy.76
  75.2 0.9 copy.80
  76.1 46.3 %all-to-all-done = f32[16,128,256]{1,2,0:T(8,128)S(1)} async-done(((f32[16,128,256]{1,2,0:T(8,128)}), f32[16,128,256]{1,2,0:T(8,128)S(1)}, u32[]{:S(2)}, u32[]{:S(2)}) %all-to-all-start) | async-done | bytes 2097184 | tf_op jit(solution)/shard_map/all_to_all | solution.py:175
  122.5 0.7 copy.82
  123.2 0.7 copy.81
  (60 shorter events, 1.3 us)
Async XLA Ops:
  0.6 4.1 %copy-start.1 = (bf16[128,128]{1,0:T(8,128)(2,1)S(1)}, bf16[128,128]{1,0:T(8,128)(2,1)}, u32[]{:S(2)}) copy-start(bf16[128,128]{1,0:T(8,128)(2,1)} %param.52) | copy-start | bytes 98308
  0.6 21.2 %copy-start.2 = (bf16[128,128]{1,0:T(8,128)(2,1)S(1)}, bf16[128,128]{1,0:T(8,128)(2,1)}, u32[]{:S(2)}) copy-start(bf16[128,128]{1,0:T(8,128)(2,1)} %param.53) | copy-start | bytes 98308
  58.9 2.9 %copy-start = (f32[128,6]{0,1:T(8,128)}, f32[128,6]{0,1:T(8,128)S(1)}, u32[]{:S(2)}) copy-start(f32[128,6]{0,1:T(8,128)S(1)} %get-tuple-element.1469) | copy-start | bytes 9220
  61.8 60.6 %all-to-all-start = ((f32[16,128,256]{1,2,0:T(8,128)}), f32[16,128,256]{1,2,0:T(8,128)S(1)}, u32[]{:S(2)}, u32[]{:S(2)}) async-start(f32[16,128,256]{1,2,0:T(8,128)} %copy.78), calls=%async_computation | async-start | bytes 4194304 | tf_op jit(solution)/shard_map/all_to_all | solution.py:175
where the time goes:
time: 124 us
  waiting for transfers between devices  46.3 us (37%)
  blocking collectives  39.9 us (32%)
  starting transfers between devices  13.2 us (11%)
  local copies, waits for them, and re-layouts  13.1 us (11%)
  matrix products  5.79 us (5%)
  other arithmetic  4.14 us (3%)
    all_to_all x1, waiting for transfers between devices, body(): lax.all_to_all(partial_sums.reshape(ctx_count, tok_rows, 2 * head_dim), '...  46.3 us
    all_gather x1, blocking collectives, body(): value_piece = lax.all_gather(value_rows, 'ctx', axis=0, tiled=True)  22.8 us
    all_gather x1, blocking collectives, body(): key_piece = lax.all_gather(key_rows, 'ctx', axis=0, tiled=True)  17.1 us
    all_to_all x1, starting transfers between devices, body(): lax.all_to_all(partial_sums.reshape(ctx_count, tok_rows, 2 * head_dim), '...  13.2 us
    dynamic_update_slice x8, local copies, waits for them, and re-layouts, backward_step(): lax.dynamic_update_slice_in_dim(partial_sums, block_sums, key_start, 0)  4.17 us
    unnamed x12, local copies, waits for them, and re-layouts  3.83 us
    reshape x1, local copies, waits for them, and re-layouts, body(): partial_sums.reshape(ctx_count, tok_rows, 2 * head_dim)  2.89 us
  transfers between devices with their start and end apart: 1, of which 1 were waited for; matrix products, arithmetic and copies ran while one was open for 1% of the time, Pallas kernels for 0%

commit v1 on v0

--- a/solution.py
+++ b/solution.py
@@ -5,6 +5,22 @@
 from jax.sharding import PartitionSpec as P
 
 PASSK = 4
+
+
+def obtain_sections(vals, device_axis, along_dim):
+    carry, mat_out = (jax.lax.axis_size(device_axis), jax.lax.axis_index(device_axis))
+    y2, earlier = (vals, 1)
+    while earlier < carry:
+        w_next = jax.lax.ppermute(
+            y2,
+            axis_name=device_axis,
+            perm=list(map(lambda dev: (dev, dev ^ earlier), range(carry))),
+        )
+        met_up = jnp.concatenate([y2, w_next], along_dim)
+        q_next = jnp.concatenate([w_next, y2], along_dim)
+        y2 = jnp.where(mat_out & earlier == 0, met_up, q_next)
+        earlier = 2 * earlier
+    return y2
 
 
 def pass_rate(correct, group_size):
@@ -94,7 +110,7 @@
     row_total = jnp.zeros((tok_rows, head_count), jnp.float32)
     weighted = jnp.zeros((tok_rows, head_count), jnp.float32)
     key_piece = lax.all_gather(key_rows, "ctx", axis=0, tiled=True)
-    value_piece = lax.all_gather(value_rows, "ctx", axis=0, tiled=True)
+    value_piece = obtain_sections(value_rows, "ctx", 0)
     piece_rows = key_piece.shape[0]
     block_rows = math.gcd(piece_rows, 512)
 

time: 124 us -> 117 us (0.944)
  blocking collectives: 39.9 us -> 23.8 us
  waiting for transfers between devices: 46.3 us -> 51.5 us
  starting transfers between devices: 13.2 us -> 15.9 us
    all_gather x1 -> x0, blocking collectives: 22.8 us -> none  [body(): value_piece = lax.all_gather(value_rows, 'ctx', axis=0, tiled=True)]
    all_gather x1, blocking collectives: 17.1 us -> 23.8 us  [body(): key_piece = lax.all_gather(key_rows, 'ctx', axis=0, tiled=True)]
    ppermute x0 -> x4, waiting for transfers between devices: none -> 5.13 us  [obtain_sections(): jax.lax.ppermute(y2, axis_name=device_axis, perm=list(map(lambda dev: (de...]
    ppermute x0 -> x4, starting transfers between devices: none -> 3.64 us  [obtain_sections(): jax.lax.ppermute(y2, axis_name=device_axis, perm=list(map(lambda dev: (de...]
  transfers between devices with their start and end apart: 1 -> 5, of which waited for: 1 -> 4; matrix products, arithmetic and copies ran while one was open for 1% -> 4% of each run, Pallas kernels for 0% -> 0%
where the time goes in v1:
time: 117 us; the launch traced here: 116 us
  waiting for transfers between devices  51.5 us (44%)
  blocking collectives  23.8 us (20%)
  starting transfers between devices  15.9 us (14%)
  local copies, waits for them, and re-layouts  12.1 us (10%)
  matrix products  5.79 us (5%)
  other arithmetic  5.23 us (4%)
    all_to_all x1, waiting for transfers between devices, body(): lax.all_to_all(partial_sums.reshape(ctx_count, tok_rows, 2 * head_dim), '...  46.3 us
    all_gather x1, blocking collectives, body(): key_piece = lax.all_gather(key_rows, 'ctx', axis=0, tiled=True)  23.8 us
    all_to_all x1, starting transfers between devices, body(): lax.all_to_all(partial_sums.reshape(ctx_count, tok_rows, 2 * head_dim), '...  12.3 us
    ppermute x4, waiting for transfers between devices, obtain_sections(): jax.lax.ppermute(y2, axis_name=device_axis, perm=list(map(lambda dev: (de...  5.13 us
    dynamic_update_slice x8, local copies, waits for them, and re-layouts, backward_step(): lax.dynamic_update_slice_in_dim(partial_sums, block_sums, key_start, 0)  4.17 us
    ppermute x4, starting transfers between devices, obtain_sections(): jax.lax.ppermute(y2, axis_name=device_axis, perm=list(map(lambda dev: (de...  3.64 us
    unnamed x12, local copies, waits for them, and re-layouts  2.89 us
    reshape x1, local copies, waits for them, and re-layouts, body(): partial_sums.reshape(ctx_count, tok_rows, 2 * head_dim)  2.89 us
  transfers between devices with their start and end apart: 5, of which 4 were waited for; matrix products, arithmetic and copies ran while one was open for 4% of the time, Pallas kernels for 0%

profile of v1, /device:TPU:13, one launch (start us, length us, event | category | flops | bytes accessed | tf_op | source)
XLA Modules:
  0.0 116.0 jit_solution(1207560581426372436)
XLA Ops:
  0.7 0.7 collective-permute-start
  1.4 0.7 fusion.61
  2.1 0.4 collective-permute-done
  2.5 0.9 maximum_select_fusion.3
  3.3 0.3 collective-permute-start.1
  3.6 0.7 select_reduce_fusion.3
  4.4 2.1 %collective-permute-done.1 = bf16[256,128]{1,0:T(8,128)(2,1)S(1)} collective-permute-done((bf16[256,128]{1,0:T(8,128)(2,1)S(1)}, bf16[256,128]{1,0:T(8,128)(2,1)S(1)}, u32[]{:S(2)}, u32[]{:S(2)}) %collective-permute-start.1) | collective-permute-done | bytes 65568 | tf_op jit(solution)/shard_map/ppermute | solution.py:14
  6.5 0.2 collective-permute-start.2
  6.8 1.0 multiply_convert_fusion.1
  7.8 2.6 %collective-permute-done.2 = bf16[512,128]{1,0:T(8,128)(2,1)S(1)} collective-permute-done((bf16[512,128]{1,0:T(8,128)(2,1)S(1)}, bf16[512,128]{1,0:T(8,128)(2,1)S(1)}, u32[]{:S(2)}, u32[]{:S(2)}) %collective-permute-start.2) | collective-permute-done | bytes 131104 | tf_op jit(solution)/shard_map/ppermute | solution.py:14
  10.5 2.4 %collective-permute-start.3 = (bf16[1024,128]{1,0:T(8,128)(2,1)S(1)}, bf16[1024,128]{1,0:T(8,128)(2,1)S(1)}, u32[]{:S(2)}, u32[]{:S(2)}) collective-permute-start(bf16[1024,128]{1,0:T(8,128)(2,1)S(1)} %maximum_select_fusion.1), channel_id=1, source_target_pairs={{0,16},{2,18},{4,20},{6,22},{8,24},{10,26},{12,28},{14,30},{16,0},... | collective-permute-start | bytes 786440 | tf_op jit(solution)/shard_map/ppermute | solution.py:14
  13.7 23.8 %all_gather.3 = bf16[2048,128]{1,0:T(8,128)(2,1)S(1)} all-gather(bf16[128,128]{1,0:T(8,128)(2,1)S(1)} %copy-done.2), channel_id=1, replica_groups=mesh['ctx'=16,'head'=2] {'ctx'}, dimensions={0}, use_global_device_ids=true | all-gather | bytes 557056 | tf_op jit(solution)/shard_map/all_gather | solution.py:112
  37.6 3.9 %while.53 = (s32[]{:T(128)}, f32[128,6]{0,1:T(8,128)S(1)}, f32[128,6]{0,1:T(8,128)S(1)}, f32[128,6]{0,1:T(8,128)S(1)}, s32[]{:T(128)}, /*index=5*/s32[]{:T(128)}...) while((s32[]{:T(128)}, f32[128,6]{0,1:T(8,128)S(1)}, ...), condition=%wide.region_15.16_spmd.clone, body=%wide.region_1.15_spmd.clone.sunk | while | flops 205327120 | bytes 6221379 | solution.py:123
  37.7 1.7 %conditional.6 = ((f32[128,6]{0,1:T(8,128)S(1)}, f32[128,6]{0,1:T(8,128)S(1)}, f32[128,6]{0,1:T(8,128)S(1)})) conditional(s32[]{:T(128)} %clamp.18, (f32[128,6]{0,1:T(8,128)S(1)}, f32[128,6]{0,1:T(8,128)S(1)}, f32[128,6]{0,1:T(8,128)S(1)}) %tuple.202, (f32[128,6]{0,1:T(8,128)S(1)}, s32[]{:T(128)}, s32[]{:T(128)}, ...), branch_computations={%region_2.2_spmd, %region_3.6_spmd, %region_7.10_spmd, %region_11.... | conditional | flops 205327104 | bytes 5696036 | solution.py:77
  37.9 0.5 select_reduce_fusion.2
  38.3 0.6 multiply_reduce_fusion
  38.9 0.5 fusion.20
  39.5 1.7 %conditional.6 = ((f32[128,6]{0,1:T(8,128)S(1)}, f32[128,6]{0,1:T(8,128)S(1)}, f32[128,6]{0,1:T(8,128)S(1)})) conditional(s32[]{:T(128)} %clamp.18, (f32[128,6]{0,1:T(8,128)S(1)}, f32[128,6]{0,1:T(8,128)S(1)}, f32[128,6]{0,1:T(8,128)S(1)}) %tuple.202, (f32[128,6]{0,1:T(8,128)S(1)}, s32[]{:T(128)}, s32[]{:T(128)}, ...), branch_computations={%region_2.2_spmd, %region_3.6_spmd, %region_7.10_spmd, %region_11.... | conditional | flops 205327104 | bytes 5696036 | solution.py:77
  39.7 0.5 select_reduce_fusion.2
  40.2 0.6 multiply_reduce_fusion
  40.7 0.5 fusion.20
  41.6 1.5 %broadcast_in_dim.124.clone = f32[2048,256]{1,0:T(8,128)} broadcast(f32[]{:T(128)} %constant.491.clone.1), dimensions={} | broadcast | bytes 2097156 | tf_op jit(solution)/shard_map/broadcast_in_dim | solution.py:188
  43.1 8.7 %while.54 = (s32[]{:T(128)}, f32[128,6,128]{2,0,1:T(8,128)S(1)}, f32[2048,256]{1,0:T(8,128)}, s32[]{:T(128)}, s32[]{:T(128)}, /*index=5*/bf16[2048,128]{1,0:T(8,...) while((s32[]{:T(128)}, f32[128,6,128]{2,0,1:T(8,128)S(1)}, ...), condition=%wide.region_21.22_spmd.clone, body=%wide.region_16.0_spmd.clone.sunk | while | flops 506528256 | bytes 13381159 | solution.py:184
  43.1 2.1 %conditional.7 = (f32[128,6,128]{2,0,1:T(8,128)S(1)}, f32[512,256]{0,1:T(8,128)S(1)}) conditional(s32[]{:T(128)} %clamp.19, f32[128,6,128]{2,0,1:T(8,128)S(1)} %get-tuple-element.1421, (f32[128,6,128]{2,0,1:T(8,128)S(1)}, s32[]{:T(128)}, s32[]{:T(128)}, bf16[128,6,128]{0,2,1:T(8,128)(2,1)S(1)}, ...), branch_computations={%region_17.17_spmd, %region_18.18_spmd, %region_19.19_spmd, %regio... | conditional | flops 506528256 | bytes 10758676 | solution.py:77
  43.2 0.5 exponential_select_fusion.3
  43.8 0.3 convolution_bitcast_fusion.4
  44.1 0.4 multiply_convert_fusion
  44.5 0.3 fusion.56
  44.7 0.4 fusion.55
  45.2 0.2 copy.91
  45.4 0.8 constant_dynamic-update-slice_fusion.2
  46.3 2.1 %conditional.7 = (f32[128,6,128]{2,0,1:T(8,128)S(1)}, f32[512,256]{0,1:T(8,128)S(1)}) conditional(s32[]{:T(128)} %clamp.19, f32[128,6,128]{2,0,1:T(8,128)S(1)} %get-tuple-element.1421, (f32[128,6,128]{2,0,1:T(8,128)S(1)}, s32[]{:T(128)}, s32[]{:T(128)}, bf16[128,6,128]{0,2,1:T(8,128)(2,1)S(1)}, ...), branch_computations={%region_17.17_spmd, %region_18.18_spmd, %region_19.19_spmd, %regio... | conditional | flops 506528256 | bytes 10758676 | solution.py:77
  46.4 0.5 exponential_select_fusion.3
  47.0 0.3 convolution_bitcast_fusion.4
  47.2 0.4 multiply_convert_fusion
  47.6 0.3 fusion.56
  47.9 0.4 fusion.55
  48.4 0.2 copy.91
  48.6 0.9 constant_dynamic-update-slice_fusion.2
  49.7 0.9 constant_dynamic-update-slice_fusion.2
  50.7 0.2 copy.91
  50.9 0.9 constant_dynamic-update-slice_fusion.2
  51.8 2.9 %copy.78 = f32[16,128,256]{1,2,0:T(8,128)} copy(f32[16,128,256]{2,1,0:T(8,128)} %bitcast.88) | data formatting | bytes 4194304 | tf_op jit(solution)/shard_map/reshape | solution.py:192
  54.7 12.3 %all-to-all-start = ((f32[16,128,256]{1,2,0:T(8,128)}), f32[16,128,256]{1,2,0:T(8,128)S(1)}, u32[]{:S(2)}, u32[]{:S(2)}) async-start(f32[16,128,256]{1,2,0:T(8,128)} %copy.78), calls=%async_computation | async-start | bytes 4194304 | tf_op jit(solution)/shard_map/all_to_all | solution.py:191
  67.1 0.9 copy.80
  68.1 46.3 %all-to-all-done = f32[16,128,256]{1,2,0:T(8,128)S(1)} async-done(((f32[16,128,256]{1,2,0:T(8,128)}), f32[16,128,256]{1,2,0:T(8,128)S(1)}, u32[]{:S(2)}, u32[]{:S(2)}) %all-to-all-start) | async-done | bytes 2097184 | tf_op jit(solution)/shard_map/all_to_all | solution.py:191
  114.5 0.7 copy.82
  115.2 0.7 copy.81
  (71 shorter events, 2.7 us)
Async XLA Ops:
  0.6 12.7 %copy-start = (bf16[128,768]{1,0:T(8,128)(2,1)S(1)}, bf16[128,768]{1,0:T(8,128)(2,1)}, u32[]{:S(2)}) copy-start(bf16[128,768]{1,0:T(8,128)(2,1)} %param.51) | copy-start | bytes 589828
  0.6 13.0 %copy-start.2 = (bf16[128,128]{1,0:T(8,128)(2,1)S(1)}, bf16[128,128]{1,0:T(8,128)(2,1)}, u32[]{:S(2)}) copy-start(bf16[128,128]{1,0:T(8,128)(2,1)} %param.52) | copy-start | bytes 98308
  0.7 1.8 %collective-permute-start = (bf16[128,128]{1,0:T(8,128)(2,1)}, bf16[128,128]{1,0:T(8,128)(2,1)S(1)}, u32[]{:S(2)}, u32[]{:S(2)}) collective-permute-start(bf16[128,128]{1,0:T(8,128)(2,1)} %param.53), channel_id=1, source_target_pairs={{0,2},{2,0},{4,6},{6,4},{8,10},{10,8},{12,14},{14,12},{16,18},{18,... | collective-permute-start | bytes 98312 | tf_op jit(solution)/shard_map/ppermute | solution.py:14
  3.3 3.2 %collective-permute-start.1 = (bf16[256,128]{1,0:T(8,128)(2,1)S(1)}, bf16[256,128]{1,0:T(8,128)(2,1)S(1)}, u32[]{:S(2)}, u32[]{:S(2)}) collective-permute-start(bf16[256,128]{1,0:T(8,128)(2,1)S(1)} %maximum_select_fusion.3), channel_id=1, source_target_pairs={{0,4},{2,6},{4,0},{6,2},{8,12},{10,14},{12,8},{14,10},{16,20},{18,... | collective-permute-start | bytes 196616 | tf_op jit(solution)/shard_map/ppermute | solution.py:14
  6.5 3.9 %collective-permute-start.2 = (bf16[512,128]{1,0:T(8,128)(2,1)S(1)}, bf16[512,128]{1,0:T(8,128)(2,1)S(1)}, u32[]{:S(2)}, u32[]{:S(2)}) collective-permute-start(bf16[512,128]{1,0:T(8,128)(2,1)S(1)} %maximum_select_fusion.2), channel_id=1, source_target_pairs={{0,8},{2,10},{4,12},{6,14},{8,0},{10,2},{12,4},{14,6},{16,24},{18,... | collective-permute-start | bytes 393224 | tf_op jit(solution)/shard_map/ppermute | solution.py:14
  10.5 26.9 %collective-permute-start.3 = (bf16[1024,128]{1,0:T(8,128)(2,1)S(1)}, bf16[1024,128]{1,0:T(8,128)(2,1)S(1)}, u32[]{:S(2)}, u32[]{:S(2)}) collective-permute-start(bf16[1024,128]{1,0:T(8,128)(2,1)S(1)} %maximum_select_fusion.1), channel_id=1, source_target_pairs={{0,16},{2,18},{4,20},{6,22},{8,24},{10,26},{12,28},{14,30},{16,0},... | collective-permute-start | bytes 786440 | tf_op jit(solution)/shard_map/ppermute | solution.py:14
  51.8 2.9 %copy-start.1 = (f32[128,6]{0,1:T(8,128)}, f32[128,6]{0,1:T(8,128)S(1)}, u32[]{:S(2)}) copy-start(f32[128,6]{0,1:T(8,128)S(1)} %get-tuple-element.1473) | copy-start | bytes 9220
  54.7 59.7 %all-to-all-start = ((f32[16,128,256]{1,2,0:T(8,128)}), f32[16,128,256]{1,2,0:T(8,128)S(1)}, u32[]{:S(2)}, u32[]{:S(2)}) async-start(f32[16,128,256]{1,2,0:T(8,128)} %copy.78), calls=%async_computation | async-start | bytes 4194304 | tf_op jit(solution)/shard_map/all_to_all | solution.py:191
